TPU v7x, 32 devices: a whole 2x2x4 slice. The times are simulated.
32 devices in a mesh: seq: 2 (over x), ctx: 8 (over z, y), wsh: 2 (over core).
Axes of the slice: x: 2, y: 2, z: 4, core: 2. Of those that a mesh axis runs over, the one named last changes fastest.
Arguments:
- layer_in: bfloat16 [2, 1024, 896], P('seq', 'ctx'), may hold values from -6 to 6
- grad_out: bfloat16 [2, 1024, 896], P('seq', 'ctx'), may hold values from -6 to 6
- positions: int32 [2, 1024], P('seq'), may hold values from 0 to 1023, as said below
- attn_gain: bfloat16 [896], P(('seq', 'ctx', 'wsh')), may hold values from 0.099609375 to 1.8984375
- w_query: bfloat16 [896, 896], P(('seq', 'ctx'), 'wsh'), may hold values from -0.1875 to 0.1875
- b_query: bfloat16 [896], P(('seq', 'ctx', 'wsh')), may hold values from -3 to 3
- w_keyvalue: bfloat16 [896, 256], P(('seq', 'ctx'), 'wsh'), may hold values from -0.1875 to 0.1875
- b_keyvalue: bfloat16 [256], P(('seq', 'ctx', 'wsh')), may hold values from -3 to 3
- w_output: bfloat16 [896, 896], P('wsh', ('seq', 'ctx')), may hold values from -3 to 3
- mlp_gain: bfloat16 [896], P(('seq', 'ctx', 'wsh')), may hold values from 0.099609375 to 1.8984375
- w_gate: bfloat16 [896, 4864], P(('seq', 'ctx'), 'wsh'), may hold values from -0.1875 to 0.1875
- w_up: bfloat16 [896, 4864], P(('seq', 'ctx'), 'wsh'), may hold values from -0.1875 to 0.1875
- w_down: bfloat16 [4864, 896], P('wsh', ('seq', 'ctx')), may hold values from -0.078125 to 0.078125
Outputs:
- layer_out: bfloat16 [2, 1024, 896], P('seq', 'ctx')
- grad_in: bfloat16 [2, 1024, 896], P('seq', 'ctx')
- grad_attn_gain: float32 [896], P(('seq', 'ctx', 'wsh'))
- grad_w_query: float32 [896, 896], P(('seq', 'ctx'), 'wsh')
- grad_b_query: float32 [896], P(('seq', 'ctx', 'wsh'))
- grad_w_keyvalue: float32 [896, 256], P(('seq', 'ctx'), 'wsh')
- grad_b_keyvalue: float32 [256], P(('seq', 'ctx', 'wsh'))
- grad_w_output: float32 [896, 896], P('wsh', ('seq', 'ctx'))
- grad_mlp_gain: float32 [896], P(('seq', 'ctx', 'wsh'))
- grad_w_gate: float32 [896, 4864], P(('seq', 'ctx'), 'wsh')
- grad_w_up: float32 [896, 4864], P(('seq', 'ctx'), 'wsh')
- grad_w_down: float32 [4864, 896], P('wsh', ('seq', 'ctx'))
Inputs may be any that keep to these rules, and one draw needn't show every extreme that they name: Each row (one sequence) holds every position 0 to 1023 once; the 128 rows of one index of ctx are two blocks of 64 consecutive positions, block p then block 15 - p, with the pair p of each index drawn per sequence.
All inputs are finite; a program needn't handle non-finite values.
Results may differ from a plain program's by a relative error of at most 0.018.
Values may be sent and summed in bfloat16 or wider, within the bound.
No kernel may reach another device: no remote copies, remote signals or barrier semaphores. Data moves between devices by JAX's collectives and lax.ppermute only.
A program may use at most 192 MiB of HBM per device.

v0:
```python
import math

import jax
import jax.numpy as jnp
from jax import lax
from jax.sharding import PartitionSpec as P

HD = 64


epsilon = 1e-06
theta_log = math.log(1000000.0)


def partner(block, axis, stride):
    count = lax.axis_size(axis)
    route = []
    for low in range(count):
        high = low | 1 << stride
        if high != low and high < count:
            route += [(low, high), (high, low)]
    return lax.ppermute(block, axis, route)


def rope_tables(positions, half_dim):
    inv_freq = jnp.exp(-jnp.arange(half_dim, dtype=jnp.float32) * (theta_log / half_dim))
    turned = positions.astype(jnp.float32)[:, None] * inv_freq[None, :]
    return (jnp.cos(turned)[:, None, :], jnp.sin(turned)[:, None, :])


def rotate(values, cos_tab, sin_tab):
    half_dim = values.shape[-1] // 2
    first_half = values[..., :half_dim]
    second_half = values[..., half_dim:]
    return jnp.concatenate(
        [
            first_half * cos_tab - second_half * sin_tab,
            second_half * cos_tab + first_half * sin_tab,
        ],
        axis=-1,
    )


def left_inner(left_mat, right_mat):
    return lax.dot_general(
        left_mat, right_mat, (((0,), (0,)), ((), ())), preferred_element_type=jnp.float32
    )


def right_inner(left_mat, right_mat):
    return lax.dot_general(
        left_mat, right_mat, (((1,), (1,)), ((), ())), preferred_element_type=jnp.float32
    )


def norm_back(grad_normed, normed_hat, scale_inv, gain_vec):
    weighted = grad_normed * gain_vec
    return scale_inv * (
        weighted - normed_hat * jnp.mean(weighted * normed_hat, axis=-1, keepdims=True)
    )


def halve_sum(buffer, sender, group_count, group_index):
    for bit_pos in reversed(range(group_count.bit_length() - 1)):
        half_rows = buffer.shape[0] // 2
        my_bit = group_index >> bit_pos & 1
        kept_rows = lax.dynamic_slice_in_dim(buffer, my_bit * half_rows, half_rows, 0)
        outgoing = lax.dynamic_slice_in_dim(buffer, (1 - my_bit) * half_rows, half_rows, 0)
        buffer = kept_rows + sender(outgoing, bit_pos)
    return buffer


def per_device(
    layer_in,
    grad_out,
    positions,
    attn_gain,
    w_query,
    b_query,
    w_keyvalue,
    b_keyvalue,
    w_output,
    mlp_gain,
    w_gate,
    w_up,
    w_down,
):
    wq_full, wkv_full, wo_full, wg_full, wu_full, wd_full = (
        lax.all_gather(w_query, ("seq", "ctx"), axis=0, tiled=True),
        lax.all_gather(w_keyvalue, ("seq", "ctx"), axis=0, tiled=True),
        lax.all_gather(w_output, ("seq", "ctx"), axis=1, tiled=True),
        lax.all_gather(w_gate, ("seq", "ctx"), axis=0, tiled=True),
        lax.all_gather(w_up, ("seq", "ctx"), axis=0, tiled=True),
        lax.all_gather(w_down, ("seq", "ctx"), axis=1, tiled=True),
    )
    g_one, bias_q, bias_kv, g_two = (
        lax.all_gather(attn_gain, ("seq", "ctx", "wsh"), axis=0, tiled=True),
        lax.all_gather(b_query, ("seq", "ctx", "wsh"), axis=0, tiled=True),
        lax.all_gather(b_keyvalue, ("seq", "ctx", "wsh"), axis=0, tiled=True),
        lax.all_gather(mlp_gain, ("seq", "ctx", "wsh"), axis=0, tiled=True),
    )
    shard_id = lax.axis_index("wsh")
    group_count = lax.axis_size(("seq", "ctx"))
    group_index = lax.axis_index(("seq", "ctx"))
    q_cols = wq_full.shape[1]
    kv_cols = wkv_full.shape[1]
    ff_cols = wg_full.shape[1]
    bias_q = lax.dynamic_slice_in_dim(bias_q, shard_id * q_cols, q_cols).astype(jnp.float32)
    bias_kv = lax.dynamic_slice_in_dim(bias_kv, shard_id * kv_cols, kv_cols).astype(jnp.float32)
    g_one = g_one.astype(jnp.float32)
    g_two = g_two.astype(jnp.float32)
    row_count = layer_in.shape[1]
    head_count = q_cols // HD
    seq_len = positions.shape[1]
    score_scale = 1.0 / math.sqrt(HD)
    pos_all = positions[0]
    pos_mine = lax.dynamic_slice_in_dim(pos_all, lax.axis_index("ctx") * row_count, row_count)
    x_full = layer_in[0].astype(jnp.float32)
    scale_one = lax.rsqrt(jnp.mean(x_full * x_full, axis=-1, keepdims=True) + epsilon)
    hat_one = x_full * scale_one
    normed_one = (hat_one * g_one).astype(jnp.bfloat16)
    query_pre = jnp.dot(normed_one, wq_full, preferred_element_type=jnp.float32) + bias_q
    kv_pre = jnp.dot(normed_one, wkv_full, preferred_element_type=jnp.float32) + bias_kv
    cos_tab, sin_tab = rope_tables(pos_mine, HD // 2)
    query_low = rotate(query_pre.reshape(row_count, head_count, HD), cos_tab, sin_tab).astype(
        jnp.bfloat16
    )
    key_low = rotate(kv_pre[:, None, :HD], cos_tab, sin_tab)[:, 0, :].astype(jnp.bfloat16)
    value_low = kv_pre[:, HD:].astype(jnp.bfloat16)
    kv_all = lax.all_gather(
        jnp.concatenate([key_low, value_low], axis=1), "ctx", axis=0, tiled=True
    )
    k_rows = math.gcd(seq_len, 512)
    blocks_n = seq_len // k_rows
    kv_blocks = kv_all.reshape(blocks_n, k_rows, 2 * HD)
    pos_blocks = pos_all.reshape(blocks_n, k_rows)

    def block_scores(kv_block, pos_block):
        scores = (
            jnp.einsum(
                "qhd,kd->hqk", query_low, kv_block[:, :HD], preferred_element_type=jnp.float32
            )
            * score_scale
        )
        allowed = pos_block[None, :] <= pos_mine[:, None]
        return jnp.where(allowed[None], scores, -1e30)

    def stats_step(run_state, kv_pair):
        run_max, run_sum = run_state
        scores = block_scores(kv_pair[0], kv_pair[1])
        new_max = jnp.maximum(run_max, jnp.max(scores, axis=-1))
        run_sum = run_sum * jnp.exp(run_max - new_max) + jnp.sum(
            jnp.exp(scores - new_max[..., None]), axis=-1
        )
        return ((new_max, run_sum), None)

    init_max = jnp.full((head_count, row_count), -1e30, jnp.float32)
    init_sum = jnp.zeros((head_count, row_count), jnp.float32)
    (run_max, run_sum), unused = lax.scan(stats_step, (init_max, init_sum), (kv_blocks, pos_blocks))
    log_sum = run_max + jnp.log(run_sum)

    def out_step(run_state, kv_pair):
        sum_low, sum_full = run_state
        scores = block_scores(kv_pair[0], kv_pair[1])
        prob_full = jnp.exp(scores - log_sum[..., None])
        prob_low = prob_full.astype(jnp.bfloat16)
        value_blk = kv_pair[0][:, HD:]
        sum_low = sum_low + jnp.einsum(
            "hqk,kd->hqd", prob_low, value_blk, preferred_element_type=jnp.float32
        )
        sum_full = sum_full + jnp.einsum(
            "hqk,kd->hqd",
            prob_full,
            value_blk.astype(jnp.float32),
            preferred_element_type=jnp.float32,
        )
        return ((sum_low, sum_full), None)

    zero_heads = jnp.zeros((head_count, row_count, HD), jnp.float32)
    (attended, attended_exact), unused = lax.scan(
        out_step, (zero_heads, zero_heads), (kv_blocks, pos_blocks)
    )
    attended_low = (
        jnp.transpose(attended, (1, 0, 2)).reshape(row_count, head_count * HD).astype(jnp.bfloat16)
    )
    branch = lax.psum(jnp.dot(attended_low, wo_full, preferred_element_type=jnp.float32), "wsh")
    hidden = x_full + branch
    scale_two = lax.rsqrt(jnp.mean(hidden * hidden, axis=-1, keepdims=True) + epsilon)
    hat_two = hidden * scale_two
    normed_two = (hat_two * g_two).astype(jnp.bfloat16)
    gate_pre = jnp.dot(normed_two, wg_full, preferred_element_type=jnp.float32)
    up_proj = jnp.dot(normed_two, wu_full, preferred_element_type=jnp.float32)
    act_low = (jax.nn.silu(gate_pre) * up_proj).astype(jnp.bfloat16)
    mlp_out = lax.psum(
        jnp.dot(act_low, wd_full, preferred_element_type=jnp.float32).astype(jnp.bfloat16), "wsh"
    ).astype(jnp.float32)
    layer_out = (hidden + mlp_out).astype(jnp.bfloat16)
    wq_full, wkv_full, wo_full, wg_full, wu_full, wd_full = (
        lax.all_gather(w_query, ("seq", "ctx"), axis=0, tiled=True),
        lax.all_gather(w_keyvalue, ("seq", "ctx"), axis=0, tiled=True),
        lax.all_gather(w_output, ("seq", "ctx"), axis=1, tiled=True),
        lax.all_gather(w_gate, ("seq", "ctx"), axis=0, tiled=True),
        lax.all_gather(w_up, ("seq", "ctx"), axis=0, tiled=True),
        lax.all_gather(w_down, ("seq", "ctx"), axis=1, tiled=True),
    )
    grad_low = grad_out[0]
    grad_full = grad_low.astype(jnp.float32)
    grad_act = right_inner(grad_low, wd_full)
    gw_down_t = left_inner(grad_low, act_low)
    sigmoid_g = jax.nn.sigmoid(gate_pre)
    grad_up = (grad_act * (gate_pre * sigmoid_g)).astype(jnp.bfloat16)
    grad_gate = (grad_act * up_proj * sigmoid_g * (1.0 + gate_pre * (1.0 - sigmoid_g))).astype(
        jnp.bfloat16
    )
    gw_gate = left_inner(normed_two, grad_gate)
    gw_up = left_inner(normed_two, grad_up)
    part_two = right_inner(grad_gate, wg_full) + right_inner(grad_up, wu_full)
    gg_two = jnp.sum(part_two * hat_two, axis=0)
    grad_normed_two = lax.psum(part_two.astype(jnp.bfloat16), "wsh").astype(jnp.float32)
    grad_hidden = grad_full + norm_back(grad_normed_two, hat_two, scale_two, g_two)
    hidden_low = grad_hidden.astype(jnp.bfloat16)
    gw_out_t = left_inner(hidden_low, attended_low)
    grad_att = (
        right_inner(hidden_low, wo_full).reshape(row_count, head_count, HD).astype(jnp.bfloat16)
    )
    row_delta = jnp.sum(
        jnp.transpose(grad_att.astype(jnp.float32), (1, 0, 2)) * attended_exact, axis=-1
    )

    def back_step(grad_q, kv_pair):
        kv_block, pos_block = kv_pair
        scores = block_scores(kv_block, pos_block)
        prob_full = jnp.exp(scores - log_sum[..., None])
        prob_low = prob_full.astype(jnp.bfloat16)
        grad_prob = jnp.einsum(
            "qhd,kd->hqk", grad_att, kv_block[:, HD:], preferred_element_type=jnp.float32
        )
        grad_score = (prob_full * (grad_prob - row_delta[..., None])).astype(jnp.bfloat16)
        grad_q = grad_q + jnp.einsum(
            "hqk,kd->qhd", grad_score, kv_block[:, :HD], preferred_element_type=jnp.float32
        )
        grad_key = jnp.einsum(
            "hqk,qhd->kd", grad_score, query_low, preferred_element_type=jnp.float32
        )
        grad_value = jnp.einsum(
            "hqk,qhd->kd", prob_low, grad_att, preferred_element_type=jnp.float32
        )
        return (grad_q, jnp.concatenate([grad_key * score_scale, grad_value], axis=1))

    grad_q, kv_terms = lax.scan(
        back_step, jnp.zeros((row_count, head_count, HD), jnp.float32), (kv_blocks, pos_blocks)
    )
    grad_q = grad_q * score_scale
    grad_kv = lax.psum_scatter(
        kv_terms.reshape(seq_len, 2 * HD).astype(jnp.bfloat16),
        "ctx",
        scatter_dimension=0,
        tiled=True,
    ).astype(jnp.float32)
    grad_qpre = (
        rotate(grad_q, cos_tab, -sin_tab).reshape(row_count, head_count * HD).astype(jnp.bfloat16)
    )
    grad_kpre = rotate(grad_kv[:, None, :HD], cos_tab, -sin_tab)[:, 0, :]
    grad_kvpre = jnp.concatenate([grad_kpre, grad_kv[:, HD:]], axis=1).astype(jnp.bfloat16)
    gw_query = left_inner(normed_one, grad_qpre)
    gw_kv = left_inner(normed_one, grad_kvpre)
    wsh_count = lax.axis_size("wsh")
    gb_q_full = lax.dynamic_update_slice_in_dim(
        jnp.zeros((q_cols * wsh_count,), jnp.float32),
        jnp.sum(grad_qpre.astype(jnp.float32), axis=0),
        shard_id * q_cols,
        0,
    )
    gb_kv_full = lax.dynamic_update_slice_in_dim(
        jnp.zeros((kv_cols * wsh_count,), jnp.float32),
        jnp.sum(grad_kvpre.astype(jnp.float32), axis=0),
        shard_id * kv_cols,
        0,
    )
    part_one = right_inner(grad_qpre, wq_full) + right_inner(grad_kvpre, wkv_full)
    gg_one = jnp.sum(part_one * hat_one, axis=0)
    grad_normed_one = lax.psum(part_one.astype(jnp.bfloat16), "wsh").astype(jnp.float32)
    grad_input = (grad_hidden + norm_back(grad_normed_one, hat_one, scale_one, g_one)).astype(
        jnp.bfloat16
    )
    out_g_one, out_b_q, out_b_kv, out_g_two = (
        lax.psum_scatter(gg_one, ("seq", "ctx", "wsh"), scatter_dimension=0, tiled=True),
        lax.psum_scatter(gb_q_full, ("seq", "ctx", "wsh"), scatter_dimension=0, tiled=True),
        lax.psum_scatter(gb_kv_full, ("seq", "ctx", "wsh"), scatter_dimension=0, tiled=True),
        lax.psum_scatter(gg_two, ("seq", "ctx", "wsh"), scatter_dimension=0, tiled=True),
    )
    all_owned = halve_sum(
        jnp.concatenate([gw_query, gw_kv, gw_out_t, gw_gate, gw_up, gw_down_t], axis=1),
        lambda outgoing, bit_pos: partner(
            outgoing.astype(jnp.bfloat16), ("seq", "ctx"), bit_pos
        ).astype(outgoing.dtype),
        group_count,
        group_index,
    )
    proj_owned = all_owned[:, : 2 * q_cols + kv_cols]
    mlp_owned = all_owned[:, 2 * q_cols + kv_cols :]
    out_wq = proj_owned[:, :q_cols]
    out_wkv = proj_owned[:, q_cols : q_cols + kv_cols]
    out_wo = jnp.transpose(proj_owned[:, q_cols + kv_cols :])
    out_wg = mlp_owned[:, :ff_cols]
    out_wu = mlp_owned[:, ff_cols : 2 * ff_cols]
    out_wd = jnp.transpose(mlp_owned[:, 2 * ff_cols :])
    return (
        layer_out[None],
        grad_input[None],
        out_g_one,
        out_wq,
        out_b_q,
        out_wkv,
        out_b_kv,
        out_wo,
        out_g_two,
        out_wg,
        out_wu,
        out_wd,
    )


def solution(mesh):
    return jax.shard_map(
        per_device,
        mesh=mesh,
        in_specs=(
            P("seq", "ctx", None),
            P("seq", "ctx", None),
            P("seq", None),
            P(("seq", "ctx", "wsh")),
            P(("seq", "ctx"), "wsh"),
            P(("seq", "ctx", "wsh")),
            P(("seq", "ctx"), "wsh"),
            P(("seq", "ctx", "wsh")),
            P("wsh", ("seq", "ctx")),
            P(("seq", "ctx", "wsh")),
            P(("seq", "ctx"), "wsh"),
            P(("seq", "ctx"), "wsh"),
            P("wsh", ("seq", "ctx")),
        ),
        out_specs=(
            P("seq", "ctx", None),
            P("seq", "ctx", None),
            P(("seq", "ctx", "wsh")),
            P(("seq", "ctx"), "wsh"),
            P(("seq", "ctx", "wsh")),
            P(("seq", "ctx"), "wsh"),
            P(("seq", "ctx", "wsh")),
            P("wsh", ("seq", "ctx")),
            P(("seq", "ctx", "wsh")),
            P(("seq", "ctx"), "wsh"),
            P(("seq", "ctx"), "wsh"),
            P("wsh", ("seq", "ctx")),
        ),
        check_vma=False,
    )
```

profile of v0, /device:TPU:0, one launch (start us, length us, event | category | flops | bytes accessed | tf_op | source)
XLA Modules:
  0.0 1074.0 jit_solution(1286033087478032996)
XLA Ops:
  12.6 42.1 %all-reduce.9 = (bf16[256]{0:T(256)(128)(2,1)S(1)}, bf16[896]{0:T(1024)(128)(2,1)S(1)}, bf16[896]{0:T(1024)(128)(2,1)S(1)}, bf16[896]{0:T(1024)(128)(2,1)S(1)}) all-reduce(bf16[256]{0:T(256)(128)(2,1)S(1)} %dynamic-update-slice.1, bf16[896]{0:T(1024)(128)(2,1)S(1)} %dynamic-update-slice, ...), channel_id=1, replica_groups=mesh['seq'=2,'ctx'=8,'wsh'=2] {'seq','ctx','wsh'}, use_global_device_ids=true, to_apply=%add.1 | all-reduce | flops 2944 | bytes 11776
  54.7 41.0 %all_gather.40 = bf16[896,128]{1,0:T(8,128)(2,1)S(1)} all-gather(bf16[56,128]{1,0:T(8,128)(2,1)} %param.25), channel_id=1, replica_groups=mesh['seq'=2,'ctx'=8,'wsh'=2] {'seq','ctx'}, dimensions={0}, use_global_device_ids=true | all-gather | bytes 243712 | tf_op jit(solution)/shard_map/all_gather | solution.py:90
  98.2 1.3 reduce.4
  99.9 26.7 %all_gather.42 = bf16[1024,128]{0,1:T(8,128)(2,1)S(1)} all-gather(bf16[128,128]{0,1:T(8,128)(2,1)S(1)} %pad_maximum_fusion.1), channel_id=1, replica_groups=mesh['seq'=2,'ctx'=8,'wsh'=2] {'ctx'}, dimensions={0}, use_global_device_ids=true | all-gather | bytes 294912 | tf_op jit(solution)/shard_map/all_gather | solution.py:130
  126.6 42.1 %all_gather.43 = bf16[896,448]{1,0:T(8,128)(2,1)S(1)} all-gather(bf16[56,448]{1,0:T(8,128)(2,1)S(1)} %copy-done.14), channel_id=1, replica_groups=mesh['seq'=2,'ctx'=8,'wsh'=2] {'seq','ctx'}, dimensions={0}, use_global_device_ids=true | all-gather | bytes 852992 | tf_op jit(solution)/shard_map/all_gather | solution.py:89
  169.4 2.2 while.39
  171.6 2.9 while.40
  174.6 42.6 %all_gather.45 = bf16[448,896]{0,1:T(8,128)(2,1)S(1)} all-gather(bf16[448,56]{0,1:T(8,128)(2,1)S(1)} %copy-done.15), channel_id=1, replica_groups=mesh['seq'=2,'ctx'=8,'wsh'=2] {'seq','ctx'}, dimensions={1}, use_global_device_ids=true | all-gather | bytes 852992 | tf_op jit(solution)/shard_map/all_gather | solution.py:91
  220.4 13.7 %all-reduce.15.cloned.1.call-done = f32[128,896]{1,0:T(8,128)} async-done(((f32[128,896]{1,0:T(8,128)}), f32[128,896]{1,0:T(8,128)}) %all-reduce.15.cloned.1.call-update) | async-done | bytes 458768 | tf_op jit(solution)/shard_map/psum | solution.py:186
  236.1 59.4 %all-gather.6.cloned.1.call-done = bf16[896,2432]{1,0:T(8,128)(2,1)} async-done(((bf16[56,2432]{1,0:T(8,128)(2,1)}), bf16[896,2432]{1,0:T(8,128)(2,1)}) %all-gather.6.cloned.1.call-update) | async-done | bytes 4358160 | tf_op jit(solution)/shard_map/all_gather | solution.py:93
  295.5 4.3 fusion.79
  299.8 73.8 %all-gather.4.cloned.1.call-done = bf16[896,2432]{1,0:T(8,128)(2,1)} async-done(((bf16[56,2432]{1,0:T(8,128)(2,1)}), bf16[896,2432]{1,0:T(8,128)(2,1)}) %all-gather.4.cloned.1.call-update) | async-done | bytes 4358160 | tf_op jit(solution)/shard_map/all_gather | solution.py:92
  373.6 4.3 fusion.78
  377.8 73.8 %all-gather.8.cloned.1.call-done = bf16[2432,896]{0,1:T(8,128)(2,1)} async-done(((bf16[2432,56]{0,1:T(8,128)(2,1)}), bf16[2432,896]{0,1:T(8,128)(2,1)}) %all-gather.8.cloned.1.call-update) | async-done | bytes 4358160 | tf_op jit(solution)/shard_map/all_gather | solution.py:94
  451.6 5.0 multiply_convert_fusion
  456.7 5.6 fusion.83
  462.2 4.8 fusion.82
  467.0 1.3 fusion.80
  468.4 2.2 fusion.75
  470.6 5.8 convolution_bitcast_fusion.3
  476.4 11.1 %all-reduce.17.cloned.1.call-done = bf16[128,896]{1,0:T(8,128)(2,1)} async-done(((bf16[128,896]{1,0:T(8,128)(2,1)}), bf16[128,896]{1,0:T(8,128)(2,1)}) %all-reduce.17.cloned.1.call-update) | async-done | bytes 229392 | tf_op jit(solution)/shard_map/psum | solution.py:219
  487.5 1.3 multiply_reduce_fusion
  490.8 6.5 while.41
  497.3 1.8 copy.62
  499.6 1.7 fusion.34
  501.3 1.7 fusion.43
  503.1 59.5 %reduce-scatter.4.cloned.1.call-done = bf16[128,128]{1,0:T(8,128)(2,1)} async-done(((bf16[1024,128]{1,0:T(8,128)(2,1)}), bf16[128,128]{1,0:T(8,128)(2,1)}) %reduce-scatter.4.cloned.1.call-update) | async-done | bytes 32784
  564.2 35.4 %concatenate.34 = f32[896,8320]{1,0:T(8,128)} concatenate(f32[896,448]{1,0:T(8,128)} %fusion.34, f32[896,128]{1,0:T(8,128)S(1)} %fusion.63, f32[896,448]{1,0:T(8,128)} %fusion.43, f32[896,2432]{1,0:T(8,128)} %fusion.82, f32[896,2432]{1,0:T(8,128)} %fusion.83, f32[896,2432]{1,0:T(8,128)} %convolution_bitcast_fusion.3), dimensions={1} | concatenate | bytes 59637760 | tf_op jit(solution)/shard_map/concatenate | solution.py:293
  599.6 9.0 dynamic-slice_convert_fusion
  608.5 1.4 collective-permute-start
  610.0 159.1 %collective-permute-done = bf16[448,8320]{1,0:T(8,128)(2,1)} collective-permute-done((bf16[448,8320]{1,0:T(8,128)(2,1)}, bf16[448,8320]{1,0:T(8,128)(2,1)}, u32[]{:S(2)}, u32[]{:S(2)}) %collective-permute-start) | collective-permute-done | bytes 7454752 | tf_op jit(solution)/shard_map/ppermute | solution.py:22
  769.1 8.0 convert_add_fusion
  777.1 5.2 copy-done
  782.3 2.2 dynamic-slice_convert_fusion.1
  784.5 1.4 collective-permute-start.1
  785.9 159.2 %collective-permute-done.1 = bf16[224,8320]{1,0:T(8,128)(2,1)} collective-permute-done((bf16[224,8320]{1,0:T(8,128)(2,1)}, bf16[224,8320]{1,0:T(8,128)(2,1)}, u32[]{:S(2)}, u32[]{:S(2)}) %collective-permute-start.1) | collective-permute-done | bytes 3727392 | tf_op jit(solution)/shard_map/ppermute | solution.py:22
  945.1 4.9 convert_add_fusion.1
  950.0 3.0 copy-done.1
  952.9 1.4 dynamic-slice_convert_fusion.2
  954.4 4.3 convolution_convert_fusion
  960.1 36.6 %collective-permute-done.2 = bf16[112,8320]{1,0:T(8,128)(2,1)} collective-permute-done((bf16[112,8320]{1,0:T(8,128)(2,1)}, bf16[112,8320]{1,0:T(8,128)(2,1)}, u32[]{:S(2)}, u32[]{:S(2)}) %collective-permute-start.2) | collective-permute-done | bytes 1863712 | tf_op jit(solution)/shard_map/ppermute | solution.py:22
  996.6 2.9 convert_add_fusion.2
  999.6 1.8 copy-done.2
  1001.5 1.5 collective-permute-start.3
  1004.8 51.7 %all-reduce.8 = (f32[896]{0:T(1024)S(1)}, f32[896]{0:T(1024)S(1)}, f32[256]{0:T(256)S(1)}, f32[896]{0:T(1024)S(1)}) all-reduce(f32[896]{0:T(1024)S(1)} %get-tuple-element.288, f32[896]{0:T(1024)S(1)} %dynamic_update_slice.10, f32[256]{0:T(256)S(1)} %dynamic_update_slice.11, ...), channel_id=3, replica_groups=mesh['seq'=2,'ctx'=8,'wsh'=2] {'seq','ctx','wsh'}, use_global_device_ids=true, to_apply=%region_19.20.clone | all-reduce | flops 2944 | bytes 23552
  1058.8 1.7 fusion.32
  1060.5 1.8 fusion.36
  1062.3 1.7 convert_add_fusion.3
  (179 shorter events, 36.8 us)
Async XLA Ops:
  8.0 160.8 %copy-start.3 = (bf16[1,128,896]{2,1,0:T(8,128)(2,1)S(1)}, bf16[1,128,896]{2,1,0:T(8,128)(2,1)}, u32[]{:S(2)}) copy-start(bf16[1,128,896]{2,1,0:T(8,128)(2,1)} %param.19) | copy-start | bytes 688132
  8.0 118.6 %copy-start.14 = (bf16[56,448]{1,0:T(8,128)(2,1)S(1)}, bf16[56,448]{1,0:T(8,128)(2,1)}, u32[]{:S(2)}) copy-start(bf16[56,448]{1,0:T(8,128)(2,1)} %param.23) | copy-start | bytes 150532
  8.0 226.1 %all-reduce.15.cloned.1.call-start = ((), (), s32[]{:S(2)}) async-start(), calls=%async_computation.1 | async-start | bytes 917504 | tf_op jit(solution)/shard_map/psum | solution.py:186
  95.6 31.0 %copy-start.10 = (bf16[896,128]{1,0:T(8,128)(2,1)}, bf16[896,128]{1,0:T(8,128)(2,1)S(1)}, u32[]{:S(2)}) copy-start(bf16[896,128]{1,0:T(8,128)(2,1)S(1)} %all_gather.40) | copy-start | bytes 688132
  171.6 3.0 copy-start.15
  174.6 45.6 %copy-start.8 = (bf16[7,128,64]{1,2,0:T(8,128)(2,1)}, bf16[7,128,64]{1,2,0:T(8,128)(2,1)S(1)}, u32[]{:S(2)}) copy-start(bf16[7,128,64]{1,2,0:T(8,128)(2,1)S(1)} %convert_element_type.171) | copy-start | bytes 344068
  218.4 77.1 %all-gather.6.cloned.1.call-start = ((), (), s32[]{:S(2)}) async-start(), calls=%async_computation.3 | async-start | bytes 4630528 | tf_op jit(solution)/shard_map/all_gather | solution.py:93
  219.0 154.6 %all-gather.4.cloned.1.call-start = ((), (), s32[]{:S(2)}) async-start(), calls=%async_computation.2 | async-start | bytes 4630528 | tf_op jit(solution)/shard_map/all_gather | solution.py:92
  219.6 232.0 %all-gather.8.cloned.1.call-start = ((), (), s32[]{:S(2)}) async-start(), calls=%async_computation.4 | async-start | bytes 4630528 | tf_op jit(solution)/shard_map/all_gather | solution.py:94
  220.2 267.3 %all-reduce.17.cloned.1.call-start = ((), (), s32[]{:S(2)}) async-start(), calls=%async_computation.5 | async-start | bytes 458752 | tf_op jit(solution)/shard_map/psum | solution.py:219
  451.6 5.1 copy-start.4
  456.7 10.4 slice-start.2
  456.7 11.7 %slice-start = ((s8[4358144]{0:T(1024)(128)(4,1)}), s8[4194304]{0:T(1024)(128)(4,1)S(1)}, s32[]{:S(2)}) async-start(s8[4358144]{0:T(1024)(128)(4,1)} %bitcast.254), calls=%async_computation.8 | async-start | bytes 8388608
  462.2 4.8 slice-start.3
  462.2 6.1 slice-start.1
  470.6 92.0 %reduce-scatter.4.cloned.1.call-start = ((), (), s32[]{:S(2)}) async-start(), calls=%async_computation.6 | async-start | bytes 294912
  490.0 0.8 copy-start.5
  492.4 1.0 copy-start.12
  493.3 0.7 copy-start.13
  495.6 1.0 copy-start.12
  496.6 0.7 copy-start.13
  499.1 2.2 copy-start.6
  499.1 2.2 copy-start.9
  499.1 504.4 %all-reduce.19.cloned.1.call-start = ((), (), s32[]{:S(2)}) async-start(), calls=%async_computation.7 | async-start | bytes 917504 | tf_op jit(solution)/shard_map/psum | solution.py:194
  608.5 160.5 %collective-permute-start = (bf16[448,8320]{1,0:T(8,128)(2,1)}, bf16[448,8320]{1,0:T(8,128)(2,1)}, u32[]{:S(2)}, u32[]{:S(2)}) collective-permute-start(bf16[448,8320]{1,0:T(8,128)(2,1)} %dynamic-slice_convert_fusion), channel_id=1, source_target_pairs={{0,16},{16,0},{2,18},{18,2},{4,20},{20,4},{6,22},{22,6},{8,24},{24... | collective-permute-start | bytes 22364168 | tf_op jit(solution)/shard_map/ppermute | solution.py:22
  777.1 5.2 copy-start
  784.5 160.6 %collective-permute-start.1 = (bf16[224,8320]{1,0:T(8,128)(2,1)}, bf16[224,8320]{1,0:T(8,128)(2,1)}, u32[]{:S(2)}, u32[]{:S(2)}) collective-permute-start(bf16[224,8320]{1,0:T(8,128)(2,1)} %dynamic-slice_convert_fusion.1), channel_id=1, source_target_pairs={{0,8},{8,0},{2,10},{10,2},{4,12},{12,4},{6,14},{14,6},{16,24},{24,... | collective-permute-start | bytes 11182088 | tf_op jit(solution)/shard_map/ppermute | solution.py:22
  950.0 3.0 copy-start.1
  952.9 1.4 copy-start.7
  954.4 42.2 %collective-permute-start.2 = (bf16[112,8320]{1,0:T(8,128)(2,1)}, bf16[112,8320]{1,0:T(8,128)(2,1)}, u32[]{:S(2)}, u32[]{:S(2)}) collective-permute-start(bf16[112,8320]{1,0:T(8,128)(2,1)} %dynamic-slice_convert_fusion.2), channel_id=1, source_target_pairs={{0,4},{4,0},{2,6},{6,2},{8,12},{12,8},{10,14},{14,10},{16,20},{20,... | collective-permute-start | bytes 5591048 | tf_op jit(solution)/shard_map/ppermute | solution.py:22
  954.4 4.7 copy-start.11
  999.6 1.8 copy-start.2
  1001.5 60.9 %collective-permute-start.3 = (bf16[56,8320]{1,0:T(8,128)(2,1)S(1)}, bf16[56,8320]{1,0:T(8,128)(2,1)S(1)}, u32[]{:S(2)}, u32[]{:S(2)}) collective-permute-start(bf16[56,8320]{1,0:T(8,128)(2,1)S(1)} %dynamic-slice_convert_fusion.3), channel_id=1, source_target_pairs={{0,2},{2,0},{4,6},{6,4},{8,10},{10,8},{12,14},{14,12},{16,18},{18,... | collective-permute-start | bytes 2795528 | tf_op jit(solution)/shard_map/ppermute | solution.py:22
Sparse Core Ops, SparseCore 0:
  218.5 15.6 all-reduce.14
  470.7 16.7 all-reduce.16
  499.3 63.2 reduce-scatter.3
  960.2 18.2 all-reduce.18
Sparse Core Ops, SparseCore 1:
  221.7 73.8 all-gather.5
  298.2 75.3 all-gather.3
  376.2 75.3 all-gather.7
where the time goes:
time: 1080 us; the launch traced here: 1070 us
  waiting for transfers between devices  648 us (60%)
  blocking collectives  246 us (23%)
  local copies, waits for them, and re-layouts  72.7 us (7%)
  matrix products  53.7 us (5%)
  other arithmetic  32.4 us (3%)
  between operations  16 us (1%)
    ppermute x4, waiting for transfers between devices, partner(): return lax.ppermute(block, axis, route)  355 us
    unnamed x2, blocking collectives  93.8 us
    all_gather x1, waiting for transfers between devices, per_device(): lax.all_gather(w_gate, ('seq', 'ctx'), axis=0, tiled=True)  73.8 us
    all_gather x1, waiting for transfers between devices, per_device(): lax.all_gather(w_down, ('seq', 'ctx'), axis=1, tiled=True)  73.8 us
    unnamed x8, waiting for transfers between devices  61.1 us
    all_gather x1, waiting for transfers between devices, per_device(): lax.all_gather(w_up, ('seq', 'ctx'), axis=0, tiled=True)  59.4 us
    all_gather x1, blocking collectives, per_device(): lax.all_gather(w_output, ('seq', 'ctx'), axis=1, tiled=True)  42.6 us
    all_gather x1, blocking collectives, per_device(): lax.all_gather(w_query, ('seq', 'ctx'), axis=0, tiled=True)  42.1 us
  transfers between devices with their start and end apart: 11, of which 9 were waited for; matrix products, arithmetic and copies ran while one was open for 3% of the time, Pallas kernels for 0%

commit v1 on v0

--- a/solution.py
+++ b/solution.py
@@ -289,14 +289,14 @@
         lax.psum_scatter(gb_kv_full, ("seq", "ctx", "wsh"), scatter_dimension=0, tiled=True),
         lax.psum_scatter(gg_two, ("seq", "ctx", "wsh"), scatter_dimension=0, tiled=True),
     )
-    all_owned = halve_sum(
-        jnp.concatenate([gw_query, gw_kv, gw_out_t, gw_gate, gw_up, gw_down_t], axis=1),
-        lambda outgoing, bit_pos: partner(
-            outgoing.astype(jnp.bfloat16), ("seq", "ctx"), bit_pos
-        ).astype(outgoing.dtype),
-        group_count,
-        group_index,
-    )
+    all_owned = lax.psum_scatter(
+        jnp.concatenate(
+            [gw_query, gw_kv, gw_out_t, gw_gate, gw_up, gw_down_t], axis=1
+        ).astype(jnp.bfloat16),
+        ("seq", "ctx"),
+        scatter_dimension=0,
+        tiled=True,
+    ).astype(jnp.float32)
     proj_owned = all_owned[:, : 2 * q_cols + kv_cols]
     mlp_owned = all_owned[:, 2 * q_cols + kv_cols :]
     out_wq = proj_owned[:, :q_cols]

time: 1080 us -> 916 us (0.85)
  waiting for transfers between devices: 648 us -> 524 us
  local copies, waits for them, and re-layouts: 72.7 us -> 44.2 us
  other arithmetic: 32.4 us -> 14.3 us
  blocking collectives: 246 us -> 263 us
    ppermute x4 -> x0, waiting for transfers between devices: 355 us -> none  [partner(): return lax.ppermute(block, axis, route)]
    unnamed x8 -> x10, waiting for transfers between devices: 61.1 us -> 298 us
    add x4 -> x0, other arithmetic: 17.4 us -> none  [halve_sum(): buffer = kept_rows + sender(outgoing, bit_pos)]
    unnamed x2, blocking collectives: 93.8 us -> 111 us
    convert_element_type x4 -> x0, local copies, waits for them, and re-layouts: 12.7 us -> none  [per_device(): outgoing.astype(jnp.bfloat16)]
  transfers between devices with their start and end apart: 11 -> 8, of which waited for: 9 -> 7; matrix products, arithmetic and copies ran while one was open for 3% -> 7% of each run, Pallas kernels for 0% -> 0%
where the time goes in v1:
time: 916 us; the launch traced here: 915 us
  waiting for transfers between devices  524 us (57%)
  blocking collectives  263 us (29%)
  matrix products  52 us (6%)
  local copies, waits for them, and re-layouts  44.2 us (5%)
  between operations  16 us (2%)
  other arithmetic  14.3 us (2%)
    unnamed x10, waiting for transfers between devices  298 us
    unnamed x2, blocking collectives  111 us
    all_gather x1, waiting for transfers between devices, per_device(): lax.all_gather(w_down, ('seq', 'ctx'), axis=1, tiled=True)  73.9 us
    all_gather x1, waiting for transfers between devices, per_device(): lax.all_gather(w_gate, ('seq', 'ctx'), axis=0, tiled=True)  73.9 us
    all_gather x1, waiting for transfers between devices, per_device(): lax.all_gather(w_up, ('seq', 'ctx'), axis=0, tiled=True)  60.1 us
    all_gather x1, blocking collectives, per_device(): lax.all_gather(w_output, ('seq', 'ctx'), axis=1, tiled=True)  42.6 us
    all_gather x1, blocking collectives, per_device(): lax.all_gather(w_query, ('seq', 'ctx'), axis=0, tiled=True)  42.1 us
    all_gather x1, blocking collectives, per_device(): lax.all_gather(w_keyvalue, ('seq', 'ctx'), axis=0, tiled=True)  41 us
  transfers between devices with their start and end apart: 8, of which 7 were waited for; matrix products, arithmetic and copies ran while one was open for 7% of the time, Pallas kernels for 0%

profile of v1, /device:TPU:0, one launch (start us, length us, event | category | flops | bytes accessed | tf_op | source)
XLA Modules:
  0.0 914.5 jit_solution(13022958622151075140)
XLA Ops:
  8.1 1.1 fusion.30
  9.2 0.8 dynamic-update-slice.2
  10.1 0.8 dynamic-update-slice
  11.8 0.8 dynamic-update-slice.1
  12.6 42.1 %all-reduce.10 = (bf16[256]{0:T(256)(128)(2,1)S(1)}, bf16[896]{0:T(1024)(128)(2,1)S(1)}, bf16[896]{0:T(1024)(128)(2,1)S(1)}, bf16[896]{0:T(1024)(128)(2,1)S(1)}) all-reduce(bf16[256]{0:T(256)(128)(2,1)S(1)} %dynamic-update-slice.1, bf16[896]{0:T(1024)(128)(2,1)S(1)} %dynamic-update-slice, ...), channel_id=1, replica_groups=mesh['seq'=2,'ctx'=8,'wsh'=2] {'seq','ctx','wsh'}, use_global_device_ids=true, to_apply=%add.1 | all-reduce | flops 2944 | bytes 11776
  54.7 41.0 %all_gather.40 = bf16[896,128]{1,0:T(8,128)(2,1)S(1)} all-gather(bf16[56,128]{1,0:T(8,128)(2,1)} %param.25), channel_id=1, replica_groups=mesh['seq'=2,'ctx'=8,'wsh'=2] {'seq','ctx'}, dimensions={0}, use_global_device_ids=true | all-gather | bytes 243712 | tf_op jit(solution)/shard_map/all_gather | solution.py:90
  95.7 1.3 convolution_add_fusion.5
  98.2 1.3 reduce.4
  99.9 26.7 %all_gather.42 = bf16[1024,128]{0,1:T(8,128)(2,1)S(1)} all-gather(bf16[128,128]{0,1:T(8,128)(2,1)S(1)} %pad_maximum_fusion.1), channel_id=1, replica_groups=mesh['seq'=2,'ctx'=8,'wsh'=2] {'ctx'}, dimensions={0}, use_global_device_ids=true | all-gather | bytes 294912 | tf_op jit(solution)/shard_map/all_gather | solution.py:130
  126.6 42.1 %all_gather.43 = bf16[896,448]{1,0:T(8,128)(2,1)S(1)} all-gather(bf16[56,448]{1,0:T(8,128)(2,1)S(1)} %copy-done.17), channel_id=1, replica_groups=mesh['seq'=2,'ctx'=8,'wsh'=2] {'seq','ctx'}, dimensions={0}, use_global_device_ids=true | all-gather | bytes 852992 | tf_op jit(solution)/shard_map/all_gather | solution.py:89
  169.4 2.2 while.39
  171.6 2.9 while.40
  174.6 42.6 %all_gather.45 = bf16[448,896]{0,1:T(8,128)(2,1)S(1)} all-gather(bf16[448,56]{0,1:T(8,128)(2,1)S(1)} %copy-done.18), channel_id=1, replica_groups=mesh['seq'=2,'ctx'=8,'wsh'=2] {'seq','ctx'}, dimensions={1}, use_global_device_ids=true | all-gather | bytes 852992 | tf_op jit(solution)/shard_map/all_gather | solution.py:91
  217.2 1.2 fusion.74
  220.3 13.9 %all-reduce.16.cloned.1.call-done = f32[128,896]{1,0:T(8,128)} async-done(((f32[128,896]{1,0:T(8,128)}), f32[128,896]{1,0:T(8,128)}) %all-reduce.16.cloned.1.call-update) | async-done | bytes 458768 | tf_op jit(solution)/shard_map/psum | solution.py:186
  234.2 1.2 multiply_reduce_fusion.2
  235.5 60.1 %all-gather.6.cloned.1.call-done = bf16[896,2432]{1,0:T(8,128)(2,1)} async-done(((bf16[56,2432]{1,0:T(8,128)(2,1)}), bf16[896,2432]{1,0:T(8,128)(2,1)}) %all-gather.6.cloned.1.call-update) | async-done | bytes 4358160 | tf_op jit(solution)/shard_map/all_gather | solution.py:93
  295.5 4.1 fusion.76
  299.7 73.9 %all-gather.4.cloned.1.call-done = bf16[896,2432]{1,0:T(8,128)(2,1)} async-done(((bf16[56,2432]{1,0:T(8,128)(2,1)}), bf16[896,2432]{1,0:T(8,128)(2,1)}) %all-gather.4.cloned.1.call-update) | async-done | bytes 4358160 | tf_op jit(solution)/shard_map/all_gather | solution.py:92
  373.6 4.1 fusion.75
  377.7 73.9 %all-gather.8.cloned.1.call-done = bf16[2432,896]{0,1:T(8,128)(2,1)} async-done(((bf16[2432,56]{0,1:T(8,128)(2,1)}), bf16[2432,896]{0,1:T(8,128)(2,1)}) %all-gather.8.cloned.1.call-update) | async-done | bytes 4358160 | tf_op jit(solution)/shard_map/all_gather | solution.py:94
  451.6 5.0 multiply_convert_fusion
  456.6 3.4 convolution_convert_fusion.1
  460.0 1.3 fusion.77
  461.3 4.4 fusion.72
  466.0 4.6 fusion.14
  470.6 4.4 convolution_convert_fusion.6
  474.9 3.5 convolution_convert_fusion.2
  478.4 4.2 all-reduce.18.cloned.1.call-done
  482.6 1.3 multiply_reduce_fusion
  484.0 1.3 multiply_add_fusion
  485.8 1.3 convolution_convert_fusion.3
  487.1 6.6 while.41
  493.6 1.8 copy.59
  495.5 1.5 copy.50
  497.2 1.2 fusion.78
  498.4 60.5 %reduce-scatter.8.cloned.1.call-done = bf16[128,128]{1,0:T(8,128)(2,1)} async-done(((bf16[1024,128]{1,0:T(8,128)(2,1)}), bf16[128,128]{1,0:T(8,128)(2,1)}) %reduce-scatter.8.cloned.1.call-update) | async-done | bytes 32784
  558.9 0.9 fusion.71
  560.2 2.1 fusion.73
  562.4 1.3 convolution_convert_fusion.4
  563.8 1.5 copy.48
  565.7 25.7 %concatenate.35 = bf16[896,8320]{1,0:T(8,128)(2,1)} concatenate(bf16[896,448]{1,0:T(8,128)(2,1)S(1)} %copy.48, bf16[896,128]{1,0:T(8,128)(2,1)S(1)} %copy.49, bf16[896,448]{1,0:T(8,128)(2,1)S(1)} %copy.50, bf16[896,2432]{1,0:T(8,128)(2,1)} %convolution_convert_fusion.2, bf16[896,2432]{1,0:T(8,128)(2,1)} %convolution_convert_fusion.1, bf16[896,2432]{1,0:T(8,128)(2,1)} %fusion.14), dimensions={1} | concatenate | bytes 29818880 | tf_op jit(solution)/shard_map/concatenate | solution.py:293
  592.4 1.2 fusion.29
  593.6 68.7 %all-reduce.9 = (f32[896]{0:T(1024)S(1)}, f32[896]{0:T(1024)S(1)}, f32[256]{0:T(256)S(1)}, f32[896]{0:T(1024)S(1)}) all-reduce(f32[896]{0:T(1024)S(1)} %get-tuple-element.288, f32[896]{0:T(1024)S(1)} %dynamic_update_slice.10, f32[256]{0:T(256)S(1)} %dynamic_update_slice.11, ...), channel_id=3, replica_groups=mesh['seq'=2,'ctx'=8,'wsh'=2] {'seq','ctx','wsh'}, use_global_device_ids=true, to_apply=%region_19.20.clone | all-reduce | flops 2944 | bytes 23552
  664.6 2.0 fusion.33
  666.6 235.9 %reduce-scatter.10.cloned.1.call-done = bf16[56,8320]{1,0:T(8,128)(2,1)} async-done(((bf16[896,8320]{1,0:T(8,128)(2,1)}), bf16[56,8320]{1,0:T(8,128)(2,1)}) %reduce-scatter.10.cloned.1.call-update) | async-done | bytes 931856
  902.5 1.4 convert_element_type.178
  906.0 1.2 fusion.70
  (166 shorter events, 23.6 us)
Async XLA Ops:
  8.0 160.8 %copy-start.1 = (bf16[1,128,896]{2,1,0:T(8,128)(2,1)S(1)}, bf16[1,128,896]{2,1,0:T(8,128)(2,1)}, u32[]{:S(2)}) copy-start(bf16[1,128,896]{2,1,0:T(8,128)(2,1)} %param.19) | copy-start | bytes 688132
  8.0 118.6 %copy-start.17 = (bf16[56,448]{1,0:T(8,128)(2,1)S(1)}, bf16[56,448]{1,0:T(8,128)(2,1)}, u32[]{:S(2)}) copy-start(bf16[56,448]{1,0:T(8,128)(2,1)} %param.23) | copy-start | bytes 150532
  8.0 226.2 %all-reduce.16.cloned.1.call-start = ((), (), s32[]{:S(2)}) async-start(), calls=%async_computation.2 | async-start | bytes 917504 | tf_op jit(solution)/shard_map/psum | solution.py:186
  95.6 31.0 %copy-start.13 = (bf16[896,128]{1,0:T(8,128)(2,1)}, bf16[896,128]{1,0:T(8,128)(2,1)S(1)}, u32[]{:S(2)}) copy-start(bf16[896,128]{1,0:T(8,128)(2,1)S(1)} %all_gather.40) | copy-start | bytes 688132
  171.6 3.0 copy-start.18
  174.5 45.1 %copy-start.2 = (f32[7,128,64]{1,2,0:T(8,128)}, f32[7,128,64]{1,2,0:T(8,128)S(1)}, u32[]{:S(2)}) copy-start(f32[7,128,64]{1,2,0:T(8,128)S(1)} %get-tuple-element.149) | copy-start | bytes 688132
  174.6 45.6 %copy-start.11 = (bf16[7,128,64]{1,2,0:T(8,128)(2,1)}, bf16[7,128,64]{1,2,0:T(8,128)(2,1)S(1)}, u32[]{:S(2)}) copy-start(bf16[7,128,64]{1,2,0:T(8,128)(2,1)S(1)} %convert_element_type.151) | copy-start | bytes 344068
  218.4 77.1 %all-gather.6.cloned.1.call-start = ((), (), s32[]{:S(2)}) async-start(), calls=%async_computation.4 | async-start | bytes 4630528 | tf_op jit(solution)/shard_map/all_gather | solution.py:93
  219.0 154.6 %all-gather.4.cloned.1.call-start = ((), (), s32[]{:S(2)}) async-start(), calls=%async_computation.3 | async-start | bytes 4630528 | tf_op jit(solution)/shard_map/all_gather | solution.py:92
  219.6 232.0 %all-gather.8.cloned.1.call-start = ((), (), s32[]{:S(2)}) async-start(), calls=%async_computation.5 | async-start | bytes 4630528 | tf_op jit(solution)/shard_map/all_gather | solution.py:94
  220.2 262.4 %all-reduce.18.cloned.1.call-start = ((), (), s32[]{:S(2)}) async-start(), calls=%async_computation.6 | async-start | bytes 458752 | tf_op jit(solution)/shard_map/psum | solution.py:219
  456.6 3.4 copy-start.8
  456.6 3.4 copy-start
  465.7 93.2 %reduce-scatter.8.cloned.1.call-start = ((), (), s32[]{:S(2)}) async-start(), calls=%async_computation.7 | async-start | bytes 294912
  465.9 4.6 copy-start.7
  470.6 4.4 copy-start.9
  482.6 3.1 copy-start.12
  484.0 3.1 copy-start.3
  485.3 1.8 copy-start.4
  488.7 1.0 copy-start.15
  489.7 0.7 copy-start.16
  492.0 1.0 copy-start.15
  492.9 0.7 copy-start.16
  495.5 96.6 %all-reduce.20.cloned.1.call-start = ((), (), s32[]{:S(2)}) async-start(), calls=%async_computation.9 | async-start | bytes 917504 | tf_op jit(solution)/shard_map/psum | solution.py:194
  495.5 64.7 %copy-start.14 = (bf16[896,128]{1,0:T(8,128)(2,1)S(1)}, bf16[896,128]{1,0:T(8,128)(2,1)}, u32[]{:S(2)}) copy-start(bf16[896,128]{1,0:T(8,128)(2,1)} %copy-done.13) | copy-start | bytes 688132
  562.4 340.1 %reduce-scatter.10.cloned.1.call-start = ((), (), s32[]{:S(2)}) async-start(), calls=%async_computation.8 | async-start | bytes 15841280
  591.4 1.0 copy-start.10
  591.4 73.2 %copy-start.5 = (f32[128,896]{1,0:T(8,128)S(1)}, f32[128,896]{1,0:T(8,128)}, u32[]{:S(2)}) copy-start(f32[128,896]{1,0:T(8,128)} %copy-done.4) | copy-start | bytes 1376260
  902.5 2.1 copy-start.6
Sparse Core Ops, SparseCore 0:
  218.5 15.6 all-reduce.15
  465.8 16.7 all-reduce.17
  495.6 63.3 reduce-scatter.7
  562.5 17.6 all-reduce.19
Sparse Core Ops, SparseCore 1:
  221.7 73.8 all-gather.5
  298.2 75.3 all-gather.3
  376.3 75.3 all-gather.7
  591.5 310.9 reduce-scatter.9

commit v2 on v1

--- a/solution.py
+++ b/solution.py
@@ -156,7 +156,9 @@
 
     init_max = jnp.full((head_count, row_count), -1e30, jnp.float32)
     init_sum = jnp.zeros((head_count, row_count), jnp.float32)
-    (run_max, run_sum), unused = lax.scan(stats_step, (init_max, init_sum), (kv_blocks, pos_blocks))
+    (run_max, run_sum), unused = lax.scan(
+        stats_step, (init_max, init_sum), (kv_blocks, pos_blocks), unroll=True
+    )
     log_sum = run_max + jnp.log(run_sum)
 
     def out_step(run_state, kv_pair):
@@ -178,7 +180,7 @@
 
     zero_heads = jnp.zeros((head_count, row_count, HD), jnp.float32)
     (attended, attended_exact), unused = lax.scan(
-        out_step, (zero_heads, zero_heads), (kv_blocks, pos_blocks)
+        out_step, (zero_heads, zero_heads), (kv_blocks, pos_blocks), unroll=True
     )
     attended_low = (
         jnp.transpose(attended, (1, 0, 2)).reshape(row_count, head_count * HD).astype(jnp.bfloat16)
@@ -248,7 +250,8 @@
         return (grad_q, jnp.concatenate([grad_key * score_scale, grad_value], axis=1))
 
     grad_q, kv_terms = lax.scan(
-        back_step, jnp.zeros((row_count, head_count, HD), jnp.float32), (kv_blocks, pos_blocks)
+        back_step, jnp.zeros((row_count, head_count, HD), jnp.float32), (kv_blocks, pos_blocks),
+        unroll=True,
     )
     grad_q = grad_q * score_scale
     grad_kv = lax.psum_scatter(

time: 916 us -> 910 us (level)
  no operation moved by 1% of the time
where the time goes in v2:
time: 910 us; the launch traced here: 908 us
  waiting for transfers between devices  521 us (57%)
  blocking collectives  264 us (29%)
  matrix products  48.8 us (5%)
  local copies, waits for them, and re-layouts  42.4 us (5%)
  between operations  16.3 us (2%)
  other arithmetic  14.4 us (2%)
    unnamed x10, waiting for transfers between devices  298 us
    unnamed x2, blocking collectives  111 us
    all_gather x1, waiting for transfers between devices, per_device(): lax.all_gather(w_gate, ('seq', 'ctx'), axis=0, tiled=True)  73.9 us
    all_gather x1, waiting for transfers between devices, per_device(): lax.all_gather(w_down, ('seq', 'ctx'), axis=1, tiled=True)  73.9 us
    all_gather x1, waiting for transfers between devices, per_device(): lax.all_gather(w_up, ('seq', 'ctx'), axis=0, tiled=True)  60.1 us
    all_gather x1, blocking collectives, per_device(): lax.all_gather(w_output, ('seq', 'ctx'), axis=1, tiled=True)  43.2 us
    all_gather x1, blocking collectives, per_device(): lax.all_gather(w_query, ('seq', 'ctx'), axis=0, tiled=True)  42.6 us
    all_gather x1, blocking collectives, per_device(): lax.all_gather(w_keyvalue, ('seq', 'ctx'), axis=0, tiled=True)  41.1 us
  transfers between devices with their start and end apart: 8, of which 7 were waited for; matrix products, arithmetic and copies ran while one was open for 7% of the time, Pallas kernels for 0%

profile of v2, /device:TPU:0, one launch (start us, length us, event | category | flops | bytes accessed | tf_op | source)
XLA Modules:
  0.0 908.1 jit_solution(10112684432811184879)
XLA Ops:
  8.1 1.1 fusion.38
  9.3 0.8 dynamic-update-slice.2
  10.1 0.8 dynamic-update-slice
  11.0 0.8 dynamic-update-slice.3
  11.8 0.8 dynamic-update-slice.1
  12.6 42.1 %all-reduce.10 = (bf16[256]{0:T(256)(128)(2,1)S(1)}, bf16[896]{0:T(1024)(128)(2,1)S(1)}, bf16[896]{0:T(1024)(128)(2,1)S(1)}, bf16[896]{0:T(1024)(128)(2,1)}) all-reduce(bf16[256]{0:T(256)(128)(2,1)S(1)} %dynamic-update-slice.1, bf16[896]{0:T(1024)(128)(2,1)S(1)} %dynamic-update-slice, ...), channel_id=1, replica_groups=mesh['seq'=2,'ctx'=8,'wsh'=2] {'seq','ctx','wsh'}, use_global_device_ids=true, to_apply=%add.1 | all-reduce | flops 2944 | bytes 11776
  54.7 41.1 %all_gather.40 = bf16[896,128]{1,0:T(8,128)(2,1)S(1)} all-gather(bf16[56,128]{1,0:T(8,128)(2,1)} %param.19), channel_id=1, replica_groups=mesh['seq'=2,'ctx'=8,'wsh'=2] {'seq','ctx'}, dimensions={0}, use_global_device_ids=true | all-gather | bytes 243712 | tf_op jit(solution)/shard_map/all_gather | solution.py:90
  95.9 1.3 convolution_add_fusion.5
  98.5 0.7 fusion.75
  99.5 26.6 %all_gather.42 = bf16[1024,128]{0,1:T(8,128)(2,1)S(1)} all-gather(bf16[128,128]{0,1:T(8,128)(2,1)S(1)} %pad_maximum_fusion.2), channel_id=1, replica_groups=mesh['seq'=2,'ctx'=8,'wsh'=2] {'ctx'}, dimensions={0}, use_global_device_ids=true | all-gather | bytes 294912 | tf_op jit(solution)/shard_map/all_gather | solution.py:130
  126.1 42.6 %all_gather.43 = bf16[896,448]{1,0:T(8,128)(2,1)S(1)} all-gather(bf16[56,448]{1,0:T(8,128)(2,1)} %param.17), channel_id=1, replica_groups=mesh['seq'=2,'ctx'=8,'wsh'=2] {'seq','ctx'}, dimensions={0}, use_global_device_ids=true | all-gather | bytes 852992 | tf_op jit(solution)/shard_map/all_gather | solution.py:89
  168.8 43.2 %all_gather.45 = bf16[448,896]{0,1:T(8,128)(2,1)S(1)} all-gather(bf16[448,56]{0,1:T(8,128)(2,1)S(1)} %copy-done.29), channel_id=1, replica_groups=mesh['seq'=2,'ctx'=8,'wsh'=2] {'seq','ctx'}, dimensions={1}, use_global_device_ids=true | all-gather | bytes 852992 | tf_op jit(solution)/shard_map/all_gather | solution.py:91
  215.9 1.2 fusion.91
  219.0 2.7 fusion.5
  221.7 10.8 %all-reduce.16.cloned.1.call-done = f32[128,896]{1,0:T(8,128)} async-done(((f32[128,896]{1,0:T(8,128)}), f32[128,896]{1,0:T(8,128)}) %all-reduce.16.cloned.1.call-update) | async-done | bytes 458768 | tf_op jit(solution)/shard_map/psum | solution.py:188
  232.5 1.2 multiply_reduce_fusion.2
  233.8 60.1 %all-gather.6.cloned.1.call-done = bf16[896,2432]{1,0:T(8,128)(2,1)} async-done(((bf16[56,2432]{1,0:T(8,128)(2,1)}), bf16[896,2432]{1,0:T(8,128)(2,1)}) %all-gather.6.cloned.1.call-update) | async-done | bytes 4358160 | tf_op jit(solution)/shard_map/all_gather | solution.py:93
  293.9 4.1 fusion.93
  298.0 73.9 %all-gather.4.cloned.1.call-done = bf16[896,2432]{1,0:T(8,128)(2,1)} async-done(((bf16[56,2432]{1,0:T(8,128)(2,1)}), bf16[896,2432]{1,0:T(8,128)(2,1)}) %all-gather.4.cloned.1.call-update) | async-done | bytes 4358160 | tf_op jit(solution)/shard_map/all_gather | solution.py:92
  371.9 4.1 fusion.92
  376.1 73.9 %all-gather.8.cloned.1.call-done = bf16[2432,896]{0,1:T(8,128)(2,1)} async-done(((bf16[2432,56]{0,1:T(8,128)(2,1)}), bf16[2432,896]{0,1:T(8,128)(2,1)}) %all-gather.8.cloned.1.call-update) | async-done | bytes 4358160 | tf_op jit(solution)/shard_map/all_gather | solution.py:94
  450.0 4.2 multiply_convert_fusion
  454.2 3.4 convolution_convert_fusion.1
  457.5 1.3 fusion.94
  458.8 4.4 fusion.89
  463.5 4.4 fusion
  467.9 4.3 convolution_convert_fusion.6
  472.2 3.5 convolution_convert_fusion.2
  475.7 4.5 all-reduce.18.cloned.1.call-done
  480.2 1.9 multiply_reduce_fusion
  482.1 1.2 multiply_add_fusion
  489.1 0.8 copy.64
  490.0 0.8 copy.69
  490.8 0.8 multiply_subtract_fusion
  492.2 61.2 %reduce-scatter.8.cloned.1.call-done = bf16[128,128]{1,0:T(8,128)(2,1)} async-done(((bf16[1024,128]{1,0:T(8,128)(2,1)}), bf16[128,128]{1,0:T(8,128)(2,1)}) %reduce-scatter.8.cloned.1.call-update) | async-done | bytes 32784
  553.4 0.9 fusion.85
  554.7 2.0 fusion.90
  557.3 0.8 copy.67
  558.5 25.7 %concatenate.47 = bf16[896,8320]{1,0:T(8,128)(2,1)} concatenate(bf16[896,448]{1,0:T(8,128)(2,1)S(1)} %copy.67, bf16[896,128]{1,0:T(8,128)(2,1)S(1)} %copy.68, bf16[896,448]{1,0:T(8,128)(2,1)S(1)} %copy.69, bf16[896,2432]{1,0:T(8,128)(2,1)} %convolution_convert_fusion.2, bf16[896,2432]{1,0:T(8,128)(2,1)} %convolution_convert_fusion.1, bf16[896,2432]{1,0:T(8,128)(2,1)} %fusion), dimensions={1} | concatenate | bytes 29818880 | tf_op jit(solution)/shard_map/concatenate | solution.py:296
  585.3 1.2 fusion.37
  586.5 68.7 %all-reduce.9 = (f32[896]{0:T(1024)S(1)}, f32[896]{0:T(1024)S(1)}, f32[256]{0:T(256)S(1)}, f32[896]{0:T(1024)S(1)}) all-reduce(f32[896]{0:T(1024)S(1)} %get-tuple-element.14, f32[896]{0:T(1024)S(1)} %dynamic_update_slice.6, f32[256]{0:T(256)S(1)} %dynamic_update_slice.7, ...), channel_id=3, replica_groups=mesh['seq'=2,'ctx'=8,'wsh'=2] {'seq','ctx','wsh'}, use_global_device_ids=true, to_apply=%region_15.16.clone | all-reduce | flops 2944 | bytes 23552
  657.5 1.7 fusion.46
  659.2 0.9 fusion.49
  660.1 235.3 %reduce-scatter.10.cloned.1.call-done = bf16[56,8320]{1,0:T(8,128)(2,1)} async-done(((bf16[896,8320]{1,0:T(8,128)(2,1)}), bf16[56,8320]{1,0:T(8,128)(2,1)}) %reduce-scatter.10.cloned.1.call-update) | async-done | bytes 931856
  895.4 1.4 convert_element_type.185
  896.8 0.7 slice_bitcast_fusion.1
  897.5 0.8 slice_bitcast_fusion
  899.7 1.1 fusion.84
  (162 shorter events, 19.8 us)
Async XLA Ops:
  8.0 160.7 %copy-start.29 = (bf16[448,56]{0,1:T(8,128)(2,1)S(1)}, bf16[448,56]{0,1:T(8,128)(2,1)}, u32[]{:S(2)}) copy-start(bf16[448,56]{0,1:T(8,128)(2,1)} %param.21) | copy-start | bytes 150532
  8.0 224.5 %all-reduce.16.cloned.1.call-start = ((), (), s32[]{:S(2)}) async-start(), calls=%async_computation.2 | async-start | bytes 917504 | tf_op jit(solution)/shard_map/psum | solution.py:188
  8.1 203.9 %copy-start.35 = (f32[32]{0:T(128)}, f32[32]{0:T(128)S(1)}, u32[]{:S(2)}) copy-start(f32[32]{0:T(128)S(1)} %multiply_exponential_fusion) | copy-start | bytes 388
  8.1 204.0 %copy-start.3 = (bf16[1,128,896]{2,1,0:T(8,128)(2,1)S(1)}, bf16[1,128,896]{2,1,0:T(8,128)(2,1)}, u32[]{:S(2)}) copy-start(bf16[1,128,896]{2,1,0:T(8,128)(2,1)} %param.13) | copy-start | bytes 688132
  9.3 203.3 %copy-start.31 = (f32[128]{0:T(128)}, f32[128]{0:T(128)S(1)}, u32[]{:S(2)}) copy-start(f32[128]{0:T(128)S(1)} %add_rsqrt_fusion.1) | copy-start | bytes 1540
  54.7 157.9 %copy-start.25 = (f32[896]{0:T(1024)}, f32[896]{0:T(1024)S(1)}, u32[]{:S(2)}) copy-start(f32[896]{0:T(1024)S(1)} %convert_element_type.149) | copy-start | bytes 10756
  95.8 3.7 copy-start.17
  98.5 0.9 copy-start.33
  99.3 113.5 %copy-start.27 = (f32[128,32]{0,1:T(8,128)}, f32[128,32]{0,1:T(8,128)S(1)}, u32[]{:S(2)}) copy-start(f32[128,32]{0,1:T(8,128)S(1)} %get-tuple-element.53) | copy-start | bytes 49156
  126.1 92.8 %copy-start.13 = (bf16[1024,128]{0,1:T(8,128)(2,1)}, bf16[1024,128]{0,1:T(8,128)(2,1)S(1)}, u32[]{:S(2)}) copy-start(bf16[1024,128]{0,1:T(8,128)(2,1)S(1)} %all_gather.42) | copy-start | bytes 786436
  168.8 44.2 %copy-start.4 = (bf16[896,448]{1,0:T(8,128)(2,1)}, bf16[896,448]{1,0:T(8,128)(2,1)S(1)}, u32[]{:S(2)}) copy-start(bf16[896,448]{1,0:T(8,128)(2,1)S(1)} %all_gather.43) | copy-start | bytes 2408452
  212.0 3.9 copy-start.6
  212.9 0.9 copy-start.19
  212.9 0.9 copy-start.21
  213.8 1.2 copy-start
  215.1 3.9 copy-start.23
  215.9 3.0 copy-start.38
  217.1 76.8 %all-gather.6.cloned.1.call-start = ((), (), s32[]{:S(2)}) async-start(), calls=%async_computation.4 | async-start | bytes 4630528 | tf_op jit(solution)/shard_map/all_gather | solution.py:93
  217.7 154.2 %all-gather.4.cloned.1.call-start = ((), (), s32[]{:S(2)}) async-start(), calls=%async_computation.3 | async-start | bytes 4630528 | tf_op jit(solution)/shard_map/all_gather | solution.py:92
  218.3 231.7 %all-gather.8.cloned.1.call-start = ((), (), s32[]{:S(2)}) async-start(), calls=%async_computation.5 | async-start | bytes 4630528 | tf_op jit(solution)/shard_map/all_gather | solution.py:94
  218.9 261.3 %all-reduce.18.cloned.1.call-start = ((), (), s32[]{:S(2)}) async-start(), calls=%async_computation.6 | async-start | bytes 458752 | tf_op jit(solution)/shard_map/psum | solution.py:221
  219.0 14.9 %copy-start.28 = (f32[896]{0:T(1024)}, f32[896]{0:T(1024)S(1)}, u32[]{:S(2)}) copy-start(f32[896]{0:T(1024)S(1)} %convert_element_type.160) | copy-start | bytes 10756
  233.7 64.3 %copy-start.37 = (f32[128]{0:T(128)}, f32[128]{0:T(128)S(1)}, u32[]{:S(2)}) copy-start(f32[128]{0:T(128)S(1)} %add_rsqrt_fusion) | copy-start | bytes 1540
  454.2 3.4 copy-start.11
  454.2 3.4 copy-start.2
  463.3 90.1 %reduce-scatter.8.cloned.1.call-start = ((), (), s32[]{:S(2)}) async-start(), calls=%async_computation.7 | async-start | bytes 294912
  467.9 4.3 copy-start.12
  475.7 7.7 copy-start.7
  480.2 3.7 copy-start.24
  483.4 4.6 copy-start.8
  483.4 1.7 copy-start.1
  483.9 1.6 copy-start.14
  483.9 1.6 copy-start.16
  486.4 0.8 copy-start.20
  486.4 0.8 copy-start.22
  489.1 2.7 copy-start.5
  490.0 95.0 %all-reduce.20.cloned.1.call-start = ((), (), s32[]{:S(2)}) async-start(), calls=%async_computation.9 | async-start | bytes 917504 | tf_op jit(solution)/shard_map/psum | solution.py:196
  490.8 63.8 %copy-start.34 = (f32[128]{0:T(128)S(1)}, f32[128]{0:T(128)}, u32[]{:S(2)}) copy-start(f32[128]{0:T(128)} %copy-done.33) | copy-start | bytes 1540
  490.8 63.8 %copy-start.36 = (f32[32]{0:T(128)S(1)}, f32[32]{0:T(128)}, u32[]{:S(2)}) copy-start(f32[32]{0:T(128)} %copy-done.35) | copy-start | bytes 388
  491.7 65.1 %copy-start.26 = (f32[896]{0:T(1024)S(1)}, f32[896]{0:T(1024)}, u32[]{:S(2)}) copy-start(f32[896]{0:T(1024)} %copy-done.25) | copy-start | bytes 10756
  491.7 65.1 %copy-start.32 = (f32[128]{0:T(128)S(1)}, f32[128]{0:T(128)}, u32[]{:S(2)}) copy-start(f32[128]{0:T(128)} %copy-done.31) | copy-start | bytes 1540
  556.8 338.6 %reduce-scatter.10.cloned.1.call-start = ((), (), s32[]{:S(2)}) async-start(), calls=%async_computation.8 | async-start | bytes 15841280
  584.3 1.0 copy-start.15
  584.3 2.2 copy-start.30
  584.3 74.9 %copy-start.9 = (f32[128,896]{1,0:T(8,128)S(1)}, f32[128,896]{1,0:T(8,128)}, u32[]{:S(2)}) copy-start(f32[128,896]{1,0:T(8,128)} %copy-done.8) | copy-start | bytes 1376260
  584.9 74.2 %copy-start.18 = (bf16[128,896]{1,0:T(8,128)(2,1)S(1)}, bf16[128,896]{1,0:T(8,128)(2,1)}, u32[]{:S(2)}) copy-start(bf16[128,896]{1,0:T(8,128)(2,1)} %get-tuple-element.25) | copy-start | bytes 688132
  895.4 3.0 copy-start.10
Sparse Core Ops, SparseCore 0:
  217.3 15.2 all-reduce.15
  463.4 16.7 all-reduce.17
  490.1 63.2 reduce-scatter.7
  556.9 17.6 all-reduce.19
Sparse Core Ops, SparseCore 1:
  220.4 73.4 all-gather.5
  296.6 75.3 all-gather.3
  374.6 75.3 all-gather.7
  584.4 311.0 reduce-scatter.9
